TPU v7x, 256 devices: a whole 4x4x8 slice. The times are simulated.
256 devices in a mesh: ctx: 32 (over y, z), rep: 8 (over x, core).
Axes of the slice: x: 4, y: 4, z: 8, core: 2. Of those that a mesh axis runs over, the one named last changes fastest.
Arguments:
- queries: bfloat16 [32768, 4096], P(('rep', 'ctx')), parts along dimension 0, may hold values from -6 to 6
- key_rows: bfloat16 [32768, 4096], P(('rep', 'ctx')), parts along dimension 0, may hold values from -6 to 6
- value_rows: bfloat16 [32768, 4096], P(('rep', 'ctx')), parts along dimension 0, may hold values from -8 to 8
- doc_blocks: int32 [24], P('rep'), parts along dimension 0, may hold values from 1 to 16, 32 in all
- phm_mix: float32 [4, 4, 4], replicated, may hold values from -4 to 4
- phm_blocks: bfloat16 [4096, 1280], P('ctx'), may hold values from -0.09375 to 0.09375
Outputs:
- projected: bfloat16 [32768, 5120], P(('rep', 'ctx')), parts along dimension 0
There are 8 independent parts, one for each index of `rep`. A program takes and returns all parts, laid end to end along the dimension named above; an argument that names none is the same for every part. Nothing has to cross between parts.
Inputs may be any that keep to these rules, and one draw needn't show every extreme that they name: `doc_blocks`: entries sum to 32; the largest entry is exactly 16.
All inputs are finite; a program needn't handle non-finite values.
Results may differ from a plain program's by a relative error of at most 0.006.
Values may be sent and summed in bfloat16 or wider, within the bound.
No kernel may reach another device: no remote copies, remote signals or barrier semaphores. Data moves between devices by JAX's collectives and lax.ppermute only.
A program may use at most 64 MiB of HBM per device.

v0:
```python
import functools
import math

import jax
import jax.numpy as jnp
from jax import lax
from jax.experimental import pallas as pl
from jax.experimental.pallas import tpu as pltpu
from jax.sharding import PartitionSpec as P


HEAD_DIM = 128
PHM_N = 4
UNIT = 128
BQ = 512
BK = 256


def flash_kernel(ends_ref, q_ref, k_ref, v_ref, o_ref):
    i = pl.program_id(0)
    e0 = ends_ref[0]
    e1 = ends_ref[1]
    scale = 1.0 / math.sqrt(HEAD_DIM)
    per = BK // UNIT

    def doc_start(t):
        return jnp.where(t >= e1, e1, jnp.where(t >= e0, e0, 0))

    q_lo = i * BQ
    q_hi = q_lo + BQ - 1
    j_lo = doc_start(q_lo) // BK
    j_hi = q_hi // BK
    full_lo = (doc_start(q_hi) + BK - 1) // BK
    full_hi = (q_lo + 1) // BK - 1
    mid_lo = jnp.maximum(j_lo, jnp.minimum(full_lo, j_hi + 1))
    mid_hi = jnp.maximum(mid_lo, full_hi + 1)
    q = q_ref[...].reshape(BQ, HEAD_DIM)
    q_pos = q_lo + lax.broadcasted_iota(jnp.int32, (BQ, 1), 0)
    q_start = doc_start(q_pos)

    def step(j, carry, masked):
        m, l, acc = carry
        k = k_ref[pl.ds(j * per, per)].reshape(BK, HEAD_DIM)
        v = v_ref[pl.ds(j * per, per)].reshape(BK, HEAD_DIM)
        s = lax.dot_general(
            q, k, (((1,), (1,)), ((), ())), preferred_element_type=jnp.float32
        ) * scale
        if masked:
            k_pos = j * BK + lax.broadcasted_iota(jnp.int32, (1, BK), 1)
            mask = k_pos <= q_pos
            if masked == "both":
                mask = mask & (k_pos >= q_start)
            s = jnp.where(mask, s, -jnp.inf)
        m_new = jnp.maximum(m, jnp.max(s, axis=1, keepdims=True))
        p = jnp.exp(s - m_new)
        alpha = jnp.exp(m - m_new)
        l = alpha * l + jnp.sum(p, axis=1, keepdims=True)
        acc = alpha * acc + jnp.dot(
            p.astype(jnp.bfloat16), v, preferred_element_type=jnp.float32
        )
        return m_new, l, acc

    carry = (
        jnp.full((BQ, 1), -1e30, jnp.float32),
        jnp.zeros((BQ, 1), jnp.float32),
        jnp.zeros((BQ, HEAD_DIM), jnp.float32),
    )
    edge = functools.partial(step, masked="both")
    inner = functools.partial(step, masked=None)
    diagonal = functools.partial(step, masked="causal")
    carry = lax.fori_loop(j_lo, mid_lo, edge, carry)
    carry = lax.fori_loop(mid_lo, mid_hi, inner, carry)
    _, l, acc = lax.fori_loop(mid_hi, j_hi + 1, diagonal, carry)
    o_ref[...] = (acc / l).astype(o_ref.dtype)


def attend(qkv, ends):
    blocks = qkv.shape[0]
    seq = blocks * UNIT

    def whole(which):
        return pl.BlockSpec((blocks, None, UNIT, HEAD_DIM), lambda i, e: (0, which, 0, 0))

    return pl.pallas_call(
        flash_kernel,
        grid_spec=pltpu.PrefetchScalarGridSpec(
            num_scalar_prefetch=1,
            grid=(seq // BQ,),
            in_specs=[
                pl.BlockSpec((BQ // UNIT, None, UNIT, HEAD_DIM), lambda i, e: (i, 0, 0, 0)),
                whole(1),
                whole(2),
            ],
            out_specs=pl.BlockSpec((BQ, HEAD_DIM), lambda i, e: (i, 0)),
        ),
        out_shape=jax.ShapeDtypeStruct((seq, HEAD_DIM), jnp.bfloat16),
    )(ends, qkv, qkv, qkv)


def pack_kernel(q_ref, k_ref, v_ref, o_ref):
    for h in range(o_ref.shape[0]):
        for w, x_ref in enumerate((q_ref, k_ref, v_ref)):
            o_ref[h, w] = x_ref[:, h * HEAD_DIM:(h + 1) * HEAD_DIM]


def pack(queries, key_rows, value_rows):
    tok, width = queries.shape
    heads = width // HEAD_DIM
    groups = 2
    per = heads // groups
    spec = pl.BlockSpec((tok, per * HEAD_DIM), lambda g: (0, g))
    return pl.pallas_call(
        pack_kernel,
        grid=(groups,),
        in_specs=[spec, spec, spec],
        out_specs=pl.BlockSpec((per, 3, tok, HEAD_DIM), lambda g: (g, 0, 0, 0)),
        out_shape=jax.ShapeDtypeStruct((heads, 3, tok, HEAD_DIM), queries.dtype),
    )(queries, key_rows, value_rows)


def proj_kernel(mix_ref, att_ref, w_ref, o_ref, acc_ref, mixed_ref, wide_ref):
    i = pl.program_id(0)
    halves, rows, half_cols = w_ref.shape
    cols = halves * half_cols
    slots = rows // HEAD_DIM

    @pl.when(i == 0)
    def _():
        acc_ref[...] = jnp.zeros_like(acc_ref)
        for h in range(att_ref.shape[0]):
            wide_ref[h] = att_ref[h].astype(jnp.float32)

    for b in range(PHM_N):
        for s in range(slots):
            part = wide_ref[s] * mix_ref[(i * PHM_N + 0) * PHM_N + b]
            for a in range(1, PHM_N):
                part = part + wide_ref[a * slots + s] * mix_ref[(i * PHM_N + a) * PHM_N + b]
            mixed_ref[:, s * HEAD_DIM:(s + 1) * HEAD_DIM] = part.astype(jnp.bfloat16)
        mixed = mixed_ref[...]
        for h in range(halves):
            acc_ref[b, :, h * half_cols:(h + 1) * half_cols] += jnp.dot(
                mixed, w_ref[h], preferred_element_type=jnp.float32
            )

    @pl.when(i == PHM_N - 1)
    def _():
        for b in range(PHM_N):
            o_ref[:, b * cols:(b + 1) * cols] = acc_ref[b].astype(o_ref.dtype)


def project(att, mix, w):
    heads, tok, _ = att.shape
    halves, _, half_cols = w.shape
    rows = heads * HEAD_DIM // PHM_N
    cols = halves * half_cols
    return pl.pallas_call(
        proj_kernel,
        grid=(PHM_N,),
        in_specs=[
            pl.BlockSpec(memory_space=pltpu.SMEM),
            pl.BlockSpec((heads, tok, HEAD_DIM), lambda i: (0, 0, 0)),
            pl.BlockSpec((halves, rows, half_cols), lambda i: (0, i, 0)),
        ],
        out_specs=pl.BlockSpec((tok, PHM_N * cols), lambda i: (0, 0)),
        out_shape=jax.ShapeDtypeStruct((tok, PHM_N * cols), jnp.bfloat16),
        scratch_shapes=[
            pltpu.VMEM((PHM_N, tok, cols), jnp.float32),
            pltpu.VMEM((tok, rows), jnp.bfloat16),
            pltpu.VMEM((heads, tok, HEAD_DIM), jnp.float32),
        ],
    )(mix.reshape(-1), att, w)


def gather_factors(phm_blocks):
    cols = phm_blocks.shape[1]
    half = cols // lax.axis_size("core")
    mine = lax.dynamic_slice_in_dim(phm_blocks, lax.axis_index("core") * half, half, 1)
    over_ctx = lax.all_gather(mine, "ctx", axis=0, tiled=True)
    return lax.all_gather(over_ctx, "core", axis=0)


def body(queries, key_rows, value_rows, doc_blocks, phm_mix, phm_blocks):
    tok_rows = queries.shape[0]
    heads = queries.shape[1] // HEAD_DIM
    factors = gather_factors(phm_blocks)
    stacked = pack(queries, key_rows, value_rows)
    gathered = lax.all_to_all(stacked, "ctx", split_axis=0, concat_axis=0, tiled=True)
    ends = jnp.cumsum(doc_blocks.astype(jnp.int32) * UNIT).astype(jnp.int32)
    attended = attend(gathered, ends)
    returned = lax.all_to_all(
        attended.reshape(heads, tok_rows, HEAD_DIM), "ctx", split_axis=0, concat_axis=0, tiled=True
    )
    return project(returned, phm_mix, factors)


def solution(mesh):
    rep_at = mesh.axis_names.index("rep")
    shape = list(mesh.devices.shape)
    shape[rep_at:rep_at + 1] = [shape[rep_at] // 2, 2]
    names = list(mesh.axis_names)
    names[rep_at:rep_at + 1] = ["x", "core"]
    split = jax.sharding.Mesh(mesh.devices.reshape(shape), tuple(names))
    rows = P(("x", "core", "ctx"), None)
    placed = (rows, rows, rows, P(("x", "core")), P(), P("ctx", None))
    return jax.shard_map(body, mesh=split, in_specs=placed, out_specs=rows, check_vma=False)
```

profile of v0, /device:TPU:2, one launch (start us, length us, event | category | flops | bytes accessed | tf_op | source)
XLA Modules:
  0.0 260.4 jit_solution(15814074749921092984)
XLA Ops:
  6.5 0.0 copy-start
  6.5 0.0 all-gather.4.cloned.1.call-start
  6.5 1.0 copy-done
  7.5 0.7 constant_dynamic-slice_fusion
  8.2 0.0 all-gather.4.cloned.1.call-update
  8.2 0.0 all-gather.6.cloned.1.call-start
  8.3 89.5 %all-gather.4.cloned.1.call-done = bf16[4096,640]{1,0:T(8,128)(2,1)} async-done(((bf16[128,640]{1,0:T(8,128)(2,1)}), bf16[4096,640]{1,0:T(8,128)(2,1)}) %all-gather.4.cloned.1.call-update) | async-done | bytes 5242896 | tf_op jit(solution)/shard_map/all_gather | solution.py:178
  97.8 0.0 all-gather.6.cloned.1.call-update
  97.8 3.3 %shard_map.64 = bf16[32,3,128,128]{3,2,1,0:T(8,128)(2,1)} custom-call(bf16[128,4096]{1,0:T(8,128)(2,1)} %q_ref.1, bf16[128,4096]{1,0:T(8,128)(2,1)} %k_ref.1, bf16[128,4096]{1,0:T(8,128)(2,1)} %v_ref.1), custom_call_target="tpu_custom_call" | custom-call | tf_op jit(solution)/shard_map/pallas_call | solution.py:112
  101.1 0.0 copy-start.4
  101.1 5.7 %all-to-all-start = ((bf16[32,3,128,128]{3,2,1,0:T(8,128)(2,1)}), bf16[32,3,128,128]{3,2,1,0:T(8,128)(2,1)S(1)}, u32[]{:S(2)}, u32[]{:S(2)}) async-start(bf16[32,3,128,128]{3,2,1,0:T(8,128)(2,1)} %shard_map.64), calls=%async_computation | async-start | bytes 6291456 | tf_op jit(solution)/shard_map/all_to_all | solution.py:187
  106.9 0.0 copy-done.4
  106.9 0.7 reduce-window.9
  107.6 71.1 %all-to-all-done.q_ref.k_ref.v_ref = bf16[32,3,128,128]{3,2,1,0:T(8,128)(2,1)S(1)} async-done(((bf16[32,3,128,128]{3,2,1,0:T(8,128)(2,1)}), bf16[32,3,128,128]{3,2,1,0:T(8,128)(2,1)S(1)}, u32[]{:S(2)}, u32[]{:S(2)}) %all-to-all-start) | async-done | bytes 3145760 | tf_op jit(solution)/shard_map/all_to_all | solution.py:187
  178.7 0.0 copy-start.1
  178.7 1.6 copy-done.1
  180.4 0.0 copy-start.3
  180.4 26.2 %shard_map.65 = bf16[4096,128]{1,0:T(8,128)(2,1)} custom-call(s32[3]{0:T(128)} %bitcast.7, bf16[32,3,128,128]{3,2,1,0:T(8,128)(2,1)} %copy-done.1, bf16[32,3,128,128]{3,2,1,0:T(8,128)(2,1)} %copy-done.1, bf16[32,3,128,128]{3,2,1,0:T(8,128)(2,1)} %copy-done.1), custom_call_target="tpu_custom_call" | custom-call | tf_op jit(solution)/shard_map/pallas_call | solution.py:84
  206.6 4.0 %all-to-all-start.1 = ((bf16[32,128,128]{2,1,0:T(8,128)(2,1)}), bf16[32,128,128]{2,1,0:T(8,128)(2,1)S(1)}, u32[]{:S(2)}, u32[]{:S(2)}) async-start(bf16[32,128,128]{2,1,0:T(8,128)(2,1)} %bitcast.6), calls=%async_computation.1 | async-start | bytes 2097152 | tf_op jit(solution)/shard_map/all_to_all | solution.py:190
  210.6 0.0 copy-done.3
  210.6 0.7 reshape.32.mix_ref
  211.3 28.6 %all-to-all-done.1.att_ref = bf16[32,128,128]{2,1,0:T(8,128)(2,1)S(1)} async-done(((bf16[32,128,128]{2,1,0:T(8,128)(2,1)}), bf16[32,128,128]{2,1,0:T(8,128)(2,1)S(1)}, u32[]{:S(2)}, u32[]{:S(2)}) %all-to-all-start.1) | async-done | bytes 1048608 | tf_op jit(solution)/shard_map/all_to_all | solution.py:190
  239.9 0.0 copy-start.2
  239.9 0.0 all-gather.6.cloned.1.call-done
  239.9 1.0 copy-done.2
  240.9 12.6 %shard_map.66 = bf16[128,5120]{1,0:T(8,128)(2,1)} custom-call(f32[64]{0:T(128)} %reshape.32.mix_ref, bf16[32,128,128]{2,1,0:T(8,128)(2,1)} %copy-done.2, bf16[2,4096,640]{2,1,0:T(8,128)(2,1)} %bitcast.5), custom_call_target="tpu_custom_call" | custom-call | tf_op jit(solution)/shard_map/pallas_call | solution.py:156
  (1 shorter events, 0.0 us)
Async XLA Ops:
  6.5 1.0 copy-start
  6.5 91.3 %all-gather.4.cloned.1.call-start = ((), (), s32[]{:S(2)}) async-start(), calls=%async_computation.2 | async-start | bytes 5406720 | tf_op jit(solution)/shard_map/all_gather | solution.py:178
  8.2 231.7 %all-gather.6.cloned.1.call-start = ((), (), s32[]{:S(2)}) async-start(), calls=%async_computation.3 | async-start | bytes 15728640 | tf_op jit(solution)/shard_map/all_gather | solution.py:179
  101.1 5.7 %copy-start.4 = (s32[3]{0:T(128)S(1)}, s32[3]{0:T(128)}, u32[]{:S(2)}) copy-start(s32[3]{0:T(128)} %param.9) | copy-start | bytes 40
  101.1 77.6 %all-to-all-start = ((bf16[32,3,128,128]{3,2,1,0:T(8,128)(2,1)}), bf16[32,3,128,128]{3,2,1,0:T(8,128)(2,1)S(1)}, u32[]{:S(2)}, u32[]{:S(2)}) async-start(bf16[32,3,128,128]{3,2,1,0:T(8,128)(2,1)} %shard_map.64), calls=%async_computation | async-start | bytes 6291456 | tf_op jit(solution)/shard_map/all_to_all | solution.py:187
  178.7 1.6 copy-start.1
  180.4 30.3 %copy-start.3 = (f32[4,4,4]{2,1,0:T(4,128)S(1)}, f32[4,4,4]{2,1,0:T(4,128)}, u32[]{:S(2)}) copy-start(f32[4,4,4]{2,1,0:T(4,128)} %param.10) | copy-start | bytes 772
  206.6 33.4 %all-to-all-start.1 = ((bf16[32,128,128]{2,1,0:T(8,128)(2,1)}), bf16[32,128,128]{2,1,0:T(8,128)(2,1)S(1)}, u32[]{:S(2)}, u32[]{:S(2)}) async-start(bf16[32,128,128]{2,1,0:T(8,128)(2,1)} %bitcast.6), calls=%async_computation.1 | async-start | bytes 2097152 | tf_op jit(solution)/shard_map/all_to_all | solution.py:190
  239.9 1.0 copy-start.2
Sparse Core Ops, SparseCore 0:
  9.9 87.8 all-gather.3
  99.6 25.0 all-gather.5
where the time goes:
time: 261 us; the launch traced here: 260 us
  waiting for transfers between devices  189 us (72%)
  Pallas kernels  42.1 us (16%)
  between operations  13.4 us (5%)
  starting transfers between devices  9.81 us (4%)
  local copies, waits for them, and re-layouts  4.95 us (2%)
    all_gather x1, waiting for transfers between devices, gather_factors(): over_ctx = lax.all_gather(mine, 'ctx', axis=0, tiled=True)  89.5 us
    all_to_all x1, waiting for transfers between devices, body(): lax.all_to_all(stacked, 'ctx', split_axis=0, concat_axis=0, tiled=True)  71.1 us
    all_to_all x1, waiting for transfers between devices, body(): lax.all_to_all(attended.reshape(heads, tok_rows, HEAD_DIM), 'ctx', split_...  28.6 us
    pallas_call x1, Pallas kernels, attend(): pl.pallas_call(flash_kernel, grid_spec=pltpu.PrefetchScalarGridSpec(num_s...  26.2 us
    pallas_call x1, Pallas kernels, project(): pl.pallas_call(proj_kernel, grid=(PHM_N,), in_specs=[pl.BlockSpec(memory_...  12.6 us
    all_to_all x1, starting transfers between devices, body(): lax.all_to_all(stacked, 'ctx', split_axis=0, concat_axis=0, tiled=True)  5.72 us
  transfers between devices with their start and end apart: 4, of which 3 were waited for; matrix products, arithmetic and copies ran while one was open for 1% of the time, Pallas kernels for 11%

commit v1 on v0

--- a/solution.py
+++ b/solution.py
@@ -172,11 +172,8 @@
 
 
 def gather_factors(phm_blocks):
-    cols = phm_blocks.shape[1]
-    half = cols // lax.axis_size("core")
-    mine = lax.dynamic_slice_in_dim(phm_blocks, lax.axis_index("core") * half, half, 1)
-    over_ctx = lax.all_gather(mine, "ctx", axis=0, tiled=True)
-    return lax.all_gather(over_ctx, "core", axis=0)
+    over_ctx = lax.all_gather(phm_blocks, "ctx", axis=0, tiled=True)
+    return over_ctx[None]
 
 
 def body(queries, key_rows, value_rows, doc_blocks, phm_mix, phm_blocks):

time: 261 us -> 199 us (0.76)
  waiting for transfers between devices: 189 us -> 117 us
  starting transfers between devices: 9.81 us -> 20.2 us
    all_gather x2 -> x1, waiting for transfers between devices: 89.5 us -> 0.01 us  [gather_factors(): over_ctx = lax.all_gather(phm_blocks, 'ctx', axis=0, tiled=True)]
    all_to_all x1, waiting for transfers between devices: 71.1 us -> 88.6 us  [body(): lax.all_to_all(stacked, 'ctx', split_axis=0, concat_axis=0, tiled=True)]
    all_to_all x1, starting transfers between devices: 5.72 us -> 11.6 us  [body(): lax.all_to_all(stacked, 'ctx', split_axis=0, concat_axis=0, tiled=True)]
    all_to_all x1, starting transfers between devices: 4.04 us -> 8.58 us  [body(): lax.all_to_all(attended.reshape(heads, tok_rows, HEAD_DIM), 'ctx', split_...]
  transfers between devices with their start and end apart: 4 -> 3, of which waited for: 3 -> 2; matrix products, arithmetic and copies ran while one was open for 1% -> 1% of each run, Pallas kernels for 11% -> 15%
where the time goes in v1:
time: 199 us; the launch traced here: 196 us
  waiting for transfers between devices  117 us (59%)
  Pallas kernels  41.1 us (21%)
  starting transfers between devices  20.2 us (10%)
  between operations  13.4 us (7%)
  local copies, waits for them, and re-layouts  3.42 us (2%)
    all_to_all x1, waiting for transfers between devices, body(): lax.all_to_all(stacked, 'ctx', split_axis=0, concat_axis=0, tiled=True)  88.6 us
    all_to_all x1, waiting for transfers between devices, body(): lax.all_to_all(attended.reshape(heads, tok_rows, HEAD_DIM), 'ctx', split_...  28.1 us
    pallas_call x1, Pallas kernels, attend(): pl.pallas_call(flash_kernel, grid_spec=pltpu.PrefetchScalarGridSpec(num_s...  26.3 us
    all_to_all x1, starting transfers between devices, body(): lax.all_to_all(stacked, 'ctx', split_axis=0, concat_axis=0, tiled=True)  11.6 us
    pallas_call x1, Pallas kernels, project(): pl.pallas_call(proj_kernel, grid=(PHM_N,), in_specs=[pl.BlockSpec(memory_...  11.4 us
    all_to_all x1, starting transfers between devices, body(): lax.all_to_all(attended.reshape(heads, tok_rows, HEAD_DIM), 'ctx', split_...  8.58 us
  transfers between devices with their start and end apart: 3, of which 2 were waited for; matrix products, arithmetic and copies ran while one was open for 1% of the time, Pallas kernels for 15%

profile of v1, /device:TPU:2, one launch (start us, length us, event | category | flops | bytes accessed | tf_op | source)
XLA Modules:
  0.0 196.2 jit_solution(5916006883923422251)
XLA Ops:
  6.5 0.0 all-gather.2.cloned.1.call-start
  6.5 0.7 all-gather.2.cloned.1.call-update
  7.3 3.4 %shard_map.64 = bf16[32,3,128,128]{3,2,1,0:T(8,128)(2,1)} custom-call(bf16[128,4096]{1,0:T(8,128)(2,1)} %q_ref.1, bf16[128,4096]{1,0:T(8,128)(2,1)} %k_ref.1, bf16[128,4096]{1,0:T(8,128)(2,1)} %v_ref.1), custom_call_target="tpu_custom_call" | custom-call | tf_op jit(solution)/shard_map/pallas_call | solution.py:112
  10.7 0.0 copy-start.3
  10.7 11.6 %all-to-all-start = ((bf16[32,3,128,128]{3,2,1,0:T(8,128)(2,1)}), bf16[32,3,128,128]{3,2,1,0:T(8,128)(2,1)S(1)}, u32[]{:S(2)}, u32[]{:S(2)}) async-start(bf16[32,3,128,128]{3,2,1,0:T(8,128)(2,1)} %shard_map.64), calls=%async_computation | async-start | bytes 6291456 | tf_op jit(solution)/shard_map/all_to_all | solution.py:184
  22.3 0.0 copy-done.3
  22.3 0.7 reduce-window.9
  23.0 88.6 %all-to-all-done.q_ref.k_ref.v_ref = bf16[32,3,128,128]{3,2,1,0:T(8,128)(2,1)S(1)} async-done(((bf16[32,3,128,128]{3,2,1,0:T(8,128)(2,1)}), bf16[32,3,128,128]{3,2,1,0:T(8,128)(2,1)S(1)}, u32[]{:S(2)}, u32[]{:S(2)}) %all-to-all-start) | async-done | bytes 3145760 | tf_op jit(solution)/shard_map/all_to_all | solution.py:184
  111.6 0.0 copy-start
  111.6 1.7 copy-done
  113.3 0.0 copy-start.2
  113.3 26.3 %shard_map.65 = bf16[4096,128]{1,0:T(8,128)(2,1)} custom-call(s32[3]{0:T(128)} %bitcast.7, bf16[32,3,128,128]{3,2,1,0:T(8,128)(2,1)} %copy-done, bf16[32,3,128,128]{3,2,1,0:T(8,128)(2,1)} %copy-done, bf16[32,3,128,128]{3,2,1,0:T(8,128)(2,1)} %copy-done), custom_call_target="tpu_custom_call" | custom-call | tf_op jit(solution)/shard_map/pallas_call | solution.py:84
  139.6 8.6 %all-to-all-start.1 = ((bf16[32,128,128]{2,1,0:T(8,128)(2,1)}), bf16[32,128,128]{2,1,0:T(8,128)(2,1)S(1)}, u32[]{:S(2)}, u32[]{:S(2)}) async-start(bf16[32,128,128]{2,1,0:T(8,128)(2,1)} %bitcast.6), calls=%async_computation.1 | async-start | bytes 2097152 | tf_op jit(solution)/shard_map/all_to_all | solution.py:187
  148.2 0.0 copy-done.2
  148.2 0.7 reshape.32.mix_ref
  148.9 28.1 %all-to-all-done.1.att_ref = bf16[32,128,128]{2,1,0:T(8,128)(2,1)S(1)} async-done(((bf16[32,128,128]{2,1,0:T(8,128)(2,1)}), bf16[32,128,128]{2,1,0:T(8,128)(2,1)S(1)}, u32[]{:S(2)}, u32[]{:S(2)}) %all-to-all-start.1) | async-done | bytes 1048608 | tf_op jit(solution)/shard_map/all_to_all | solution.py:187
  177.0 0.0 copy-start.1
  177.0 0.0 all-gather.2.cloned.1.call-done
  177.0 1.0 copy-done.1
  177.9 11.4 %shard_map.66 = bf16[128,5120]{1,0:T(8,128)(2,1)} custom-call(f32[64]{0:T(128)} %reshape.32.mix_ref, bf16[32,128,128]{2,1,0:T(8,128)(2,1)} %copy-done.1, bf16[1,4096,1280]{2,1,0:T(8,128)(2,1)} %bitcast.5), custom_call_target="tpu_custom_call" | custom-call | tf_op jit(solution)/shard_map/pallas_call | solution.py:156
  (1 shorter events, 0.0 us)
Async XLA Ops:
  6.5 170.4 %all-gather.2.cloned.1.call-start = ((), (), s32[]{:S(2)}) async-start(), calls=%async_computation.2 | async-start | bytes 10813440 | tf_op jit(solution)/shard_map/all_gather | solution.py:175
  10.7 11.6 %copy-start.3 = (s32[3]{0:T(128)S(1)}, s32[3]{0:T(128)}, u32[]{:S(2)}) copy-start(s32[3]{0:T(128)} %param.9) | copy-start | bytes 40
  10.7 100.9 %all-to-all-start = ((bf16[32,3,128,128]{3,2,1,0:T(8,128)(2,1)}), bf16[32,3,128,128]{3,2,1,0:T(8,128)(2,1)S(1)}, u32[]{:S(2)}, u32[]{:S(2)}) async-start(bf16[32,3,128,128]{3,2,1,0:T(8,128)(2,1)} %shard_map.64), calls=%async_computation | async-start | bytes 6291456 | tf_op jit(solution)/shard_map/all_to_all | solution.py:184
  111.6 1.7 copy-start
  113.3 34.9 %copy-start.2 = (f32[4,4,4]{2,1,0:T(4,128)S(1)}, f32[4,4,4]{2,1,0:T(4,128)}, u32[]{:S(2)}) copy-start(f32[4,4,4]{2,1,0:T(4,128)} %param.10) | copy-start | bytes 772
  139.6 37.3 %all-to-all-start.1 = ((bf16[32,128,128]{2,1,0:T(8,128)(2,1)}), bf16[32,128,128]{2,1,0:T(8,128)(2,1)S(1)}, u32[]{:S(2)}, u32[]{:S(2)}) async-start(bf16[32,128,128]{2,1,0:T(8,128)(2,1)} %bitcast.6), calls=%async_computation.1 | async-start | bytes 2097152 | tf_op jit(solution)/shard_map/all_to_all | solution.py:187
  177.0 1.0 copy-start.1
Sparse Core Ops, SparseCore 0:
  9.9 147.9 all-gather.1

commit v2 on v1

--- a/solution.py
+++ b/solution.py
@@ -120,9 +120,7 @@
 
 def proj_kernel(mix_ref, att_ref, w_ref, o_ref, acc_ref, mixed_ref, wide_ref):
     i = pl.program_id(0)
-    halves, rows, half_cols = w_ref.shape
-    cols = halves * half_cols
-    slots = rows // HEAD_DIM
+    halves, slots, sub, cols = w_ref.shape
 
     @pl.when(i == 0)
     def _():
@@ -135,11 +133,12 @@
             part = wide_ref[s] * mix_ref[(i * PHM_N + 0) * PHM_N + b]
             for a in range(1, PHM_N):
                 part = part + wide_ref[a * slots + s] * mix_ref[(i * PHM_N + a) * PHM_N + b]
-            mixed_ref[:, s * HEAD_DIM:(s + 1) * HEAD_DIM] = part.astype(jnp.bfloat16)
-        mixed = mixed_ref[...]
+            part = part.astype(jnp.bfloat16)
+            for h in range(halves):
+                mixed_ref[h, :, s * sub:(s + 1) * sub] = part[:, h * sub:(h + 1) * sub]
         for h in range(halves):
-            acc_ref[b, :, h * half_cols:(h + 1) * half_cols] += jnp.dot(
-                mixed, w_ref[h], preferred_element_type=jnp.float32
+            acc_ref[b] += jnp.dot(
+                mixed_ref[h], w_ref[h].reshape(slots * sub, cols), preferred_element_type=jnp.float32
             )
 
     @pl.when(i == PHM_N - 1)
@@ -150,30 +149,32 @@
 
 def project(att, mix, w):
     heads, tok, _ = att.shape
-    halves, _, half_cols = w.shape
-    rows = heads * HEAD_DIM // PHM_N
-    cols = halves * half_cols
+    halves, shards, sub, cols = w.shape
+    slots = shards // PHM_N
     return pl.pallas_call(
         proj_kernel,
         grid=(PHM_N,),
         in_specs=[
             pl.BlockSpec(memory_space=pltpu.SMEM),
             pl.BlockSpec((heads, tok, HEAD_DIM), lambda i: (0, 0, 0)),
-            pl.BlockSpec((halves, rows, half_cols), lambda i: (0, i, 0)),
+            pl.BlockSpec((halves, slots, sub, cols), lambda i: (0, i, 0, 0)),
         ],
         out_specs=pl.BlockSpec((tok, PHM_N * cols), lambda i: (0, 0)),
         out_shape=jax.ShapeDtypeStruct((tok, PHM_N * cols), jnp.bfloat16),
         scratch_shapes=[
             pltpu.VMEM((PHM_N, tok, cols), jnp.float32),
-            pltpu.VMEM((tok, rows), jnp.bfloat16),
+            pltpu.VMEM((halves, tok, slots * sub), jnp.bfloat16),
             pltpu.VMEM((heads, tok, HEAD_DIM), jnp.float32),
         ],
     )(mix.reshape(-1), att, w)
 
 
 def gather_factors(phm_blocks):
-    over_ctx = lax.all_gather(phm_blocks, "ctx", axis=0, tiled=True)
-    return over_ctx[None]
+    rows = phm_blocks.shape[0]
+    half = rows // lax.axis_size("core")
+    mine = lax.dynamic_slice_in_dim(phm_blocks, lax.axis_index("core") * half, half, 0)
+    over_ctx = lax.all_gather(mine, "ctx", axis=0)
+    return lax.all_gather(over_ctx, "core", axis=0)
 
 
 def body(queries, key_rows, value_rows, doc_blocks, phm_mix, phm_blocks):

time: 199 us -> 259 us (1.30)
  waiting for transfers between devices: 117 us -> 189 us
  starting transfers between devices: 20.2 us -> 9.81 us
    all_gather x1 -> x2, waiting for transfers between devices: 0.01 us -> 89.5 us  [the longest x1 89.5 us: gather_factors(): over_ctx = lax.all_gather(mine, 'ctx', axis=0)]
    all_to_all x1, waiting for transfers between devices: 88.6 us -> 71.1 us  [body(): lax.all_to_all(stacked, 'ctx', split_axis=0, concat_axis=0, tiled=True)]
    all_to_all x1, starting transfers between devices: 11.6 us -> 5.72 us  [body(): lax.all_to_all(stacked, 'ctx', split_axis=0, concat_axis=0, tiled=True)]
    all_to_all x1, starting transfers between devices: 8.58 us -> 4.04 us  [body(): lax.all_to_all(attended.reshape(heads, tok_rows, HEAD_DIM), 'ctx', split_...]
  transfers between devices with their start and end apart: 3 -> 4, of which waited for: 2 -> 3; matrix products, arithmetic and copies ran while one was open for 1% -> 1% of each run, Pallas kernels for 15% -> 11%
where the time goes in v2:
time: 259 us
  waiting for transfers between devices  189 us (73%)
  Pallas kernels  40.4 us (16%)
  between operations  13.4 us (5%)
  starting transfers between devices  9.81 us (4%)
  local copies, waits for them, and re-layouts  4.94 us (2%)
    all_gather x1, waiting for transfers between devices, gather_factors(): over_ctx = lax.all_gather(mine, 'ctx', axis=0)  89.5 us
    all_to_all x1, waiting for transfers between devices, body(): lax.all_to_all(stacked, 'ctx', split_axis=0, concat_axis=0, tiled=True)  71.1 us
    all_to_all x1, waiting for transfers between devices, body(): lax.all_to_all(attended.reshape(heads, tok_rows, HEAD_DIM), 'ctx', split_...  28.6 us
    pallas_call x1, Pallas kernels, attend(): pl.pallas_call(flash_kernel, grid_spec=pltpu.PrefetchScalarGridSpec(num_s...  26.2 us
    pallas_call x1, Pallas kernels, project(): pl.pallas_call(proj_kernel, grid=(PHM_N,), in_specs=[pl.BlockSpec(memory_...  10.9 us
    all_to_all x1, starting transfers between devices, body(): lax.all_to_all(stacked, 'ctx', split_axis=0, concat_axis=0, tiled=True)  5.72 us
  transfers between devices with their start and end apart: 4, of which 3 were waited for; matrix products, arithmetic and copies ran while one was open for 1% of the time, Pallas kernels for 11%

profile of v2, /device:TPU:2, one launch (start us, length us, event | category | flops | bytes accessed | tf_op | source)
XLA Modules:
  0.0 258.7 jit_solution(1382774177611983836)
XLA Ops:
  6.5 0.0 copy-start
  6.5 0.0 all-gather.5.cloned.1.call-start
  6.5 1.0 copy-done
  7.5 0.7 constant_dynamic-slice_fusion
  8.2 0.0 all-gather.5.cloned.1.call-update
  8.2 0.0 all-gather.7.cloned.1.call-start
  8.3 89.5 %all-gather.5.cloned.1.call-done = bf16[2048,1280]{1,0:T(8,128)(2,1)} async-done(((bf16[64,1280]{1,0:T(8,128)(2,1)}), bf16[2048,1280]{1,0:T(8,128)(2,1)}) %all-gather.5.cloned.1.call-update) | async-done | bytes 5242896 | tf_op jit(solution)/shard_map/all_gather | solution.py:176
  97.8 0.0 all-gather.7.cloned.1.call-update
  97.8 3.3 %shard_map.64 = bf16[32,3,128,128]{3,2,1,0:T(8,128)(2,1)} custom-call(bf16[128,4096]{1,0:T(8,128)(2,1)} %q_ref.1, bf16[128,4096]{1,0:T(8,128)(2,1)} %k_ref.1, bf16[128,4096]{1,0:T(8,128)(2,1)} %v_ref.1), custom_call_target="tpu_custom_call" | custom-call | tf_op jit(solution)/shard_map/pallas_call | solution.py:112
  101.1 0.0 copy-start.4
  101.1 5.7 %all-to-all-start = ((bf16[32,3,128,128]{3,2,1,0:T(8,128)(2,1)}), bf16[32,3,128,128]{3,2,1,0:T(8,128)(2,1)S(1)}, u32[]{:S(2)}, u32[]{:S(2)}) async-start(bf16[32,3,128,128]{3,2,1,0:T(8,128)(2,1)} %shard_map.64), calls=%async_computation | async-start | bytes 6291456 | tf_op jit(solution)/shard_map/all_to_all | solution.py:185
  106.9 0.0 copy-done.4
  106.9 0.7 reduce-window.9
  107.6 71.1 %all-to-all-done.q_ref.k_ref.v_ref = bf16[32,3,128,128]{3,2,1,0:T(8,128)(2,1)S(1)} async-done(((bf16[32,3,128,128]{3,2,1,0:T(8,128)(2,1)}), bf16[32,3,128,128]{3,2,1,0:T(8,128)(2,1)S(1)}, u32[]{:S(2)}, u32[]{:S(2)}) %all-to-all-start) | async-done | bytes 3145760 | tf_op jit(solution)/shard_map/all_to_all | solution.py:185
  178.7 0.0 copy-start.1
  178.7 1.6 copy-done.1
  180.4 0.0 copy-start.3
  180.4 26.2 %shard_map.65 = bf16[4096,128]{1,0:T(8,128)(2,1)} custom-call(s32[3]{0:T(128)} %bitcast.9, bf16[32,3,128,128]{3,2,1,0:T(8,128)(2,1)} %copy-done.1, bf16[32,3,128,128]{3,2,1,0:T(8,128)(2,1)} %copy-done.1, bf16[32,3,128,128]{3,2,1,0:T(8,128)(2,1)} %copy-done.1), custom_call_target="tpu_custom_call" | custom-call | tf_op jit(solution)/shard_map/pallas_call | solution.py:84
  206.6 4.0 %all-to-all-start.1 = ((bf16[32,128,128]{2,1,0:T(8,128)(2,1)}), bf16[32,128,128]{2,1,0:T(8,128)(2,1)S(1)}, u32[]{:S(2)}, u32[]{:S(2)}) async-start(bf16[32,128,128]{2,1,0:T(8,128)(2,1)} %bitcast.8), calls=%async_computation.1 | async-start | bytes 2097152 | tf_op jit(solution)/shard_map/all_to_all | solution.py:188
  210.6 0.0 copy-done.3
  210.6 0.7 reshape.32.mix_ref
  211.3 28.6 %all-to-all-done.1.att_ref = bf16[32,128,128]{2,1,0:T(8,128)(2,1)S(1)} async-done(((bf16[32,128,128]{2,1,0:T(8,128)(2,1)}), bf16[32,128,128]{2,1,0:T(8,128)(2,1)S(1)}, u32[]{:S(2)}, u32[]{:S(2)}) %all-to-all-start.1) | async-done | bytes 1048608 | tf_op jit(solution)/shard_map/all_to_all | solution.py:188
  239.9 0.0 copy-start.2
  239.9 0.0 all-gather.7.cloned.1.call-done
  239.9 1.0 copy-done.2
  240.9 10.9 %shard_map.66 = bf16[128,5120]{1,0:T(8,128)(2,1)} custom-call(f32[64]{0:T(128)} %reshape.32.mix_ref, bf16[32,128,128]{2,1,0:T(8,128)(2,1)} %copy-done.2, bf16[2,32,64,1280]{3,2,1,0:T(8,128)(2,1)} %bitcast.6), custom_call_target="tpu_custom_call" | custom-call | tf_op jit(solution)/shard_map/pallas_call | solution.py:154
  (1 shorter events, 0.0 us)
Async XLA Ops:
  6.5 1.0 copy-start
  6.5 91.3 %all-gather.5.cloned.1.call-start = ((), (), s32[]{:S(2)}) async-start(), calls=%async_computation.2 | async-start | bytes 5406720 | tf_op jit(solution)/shard_map/all_gather | solution.py:176
  8.2 231.7 %all-gather.7.cloned.1.call-start = ((), (), s32[]{:S(2)}) async-start(), calls=%async_computation.3 | async-start | bytes 15728640 | tf_op jit(solution)/shard_map/all_gather | solution.py:177
  101.1 5.7 %copy-start.4 = (s32[3]{0:T(128)S(1)}, s32[3]{0:T(128)}, u32[]{:S(2)}) copy-start(s32[3]{0:T(128)} %param.9) | copy-start | bytes 40
  101.1 77.6 %all-to-all-start = ((bf16[32,3,128,128]{3,2,1,0:T(8,128)(2,1)}), bf16[32,3,128,128]{3,2,1,0:T(8,128)(2,1)S(1)}, u32[]{:S(2)}, u32[]{:S(2)}) async-start(bf16[32,3,128,128]{3,2,1,0:T(8,128)(2,1)} %shard_map.64), calls=%async_computation | async-start | bytes 6291456 | tf_op jit(solution)/shard_map/all_to_all | solution.py:185
  178.7 1.6 copy-start.1
  180.4 30.3 %copy-start.3 = (f32[4,4,4]{2,1,0:T(4,128)S(1)}, f32[4,4,4]{2,1,0:T(4,128)}, u32[]{:S(2)}) copy-start(f32[4,4,4]{2,1,0:T(4,128)} %param.10) | copy-start | bytes 772
  206.6 33.4 %all-to-all-start.1 = ((bf16[32,128,128]{2,1,0:T(8,128)(2,1)}), bf16[32,128,128]{2,1,0:T(8,128)(2,1)S(1)}, u32[]{:S(2)}, u32[]{:S(2)}) async-start(bf16[32,128,128]{2,1,0:T(8,128)(2,1)} %bitcast.8), calls=%async_computation.1 | async-start | bytes 2097152 | tf_op jit(solution)/shard_map/all_to_all | solution.py:188
  239.9 1.0 copy-start.2
Sparse Core Ops, SparseCore 0:
  9.9 87.8 all-gather.4
  99.6 25.0 all-gather.6

commit v3 on v2

--- a/solution.py
+++ b/solution.py
@@ -20,7 +20,7 @@
     i = pl.program_id(0)
     e0 = ends_ref[0]
     e1 = ends_ref[1]
-    scale = 1.0 / math.sqrt(HEAD_DIM)
+    scale = math.log2(math.e) / math.sqrt(HEAD_DIM)
     per = BK // UNIT
 
     def doc_start(t):
@@ -52,8 +52,8 @@
                 mask = mask & (k_pos >= q_start)
             s = jnp.where(mask, s, -jnp.inf)
         m_new = jnp.maximum(m, jnp.max(s, axis=1, keepdims=True))
-        p = jnp.exp(s - m_new)
-        alpha = jnp.exp(m - m_new)
+        p = jnp.exp2(s - m_new)
+        alpha = jnp.exp2(m - m_new)
         l = alpha * l + jnp.sum(p, axis=1, keepdims=True)
         acc = alpha * acc + jnp.dot(
             p.astype(jnp.bfloat16), v, preferred_element_type=jnp.float32

time: 259 us -> 259 us (level)
  no operation moved by 1% of the time
where the time goes in v3:
time: 259 us
  waiting for transfers between devices  189 us (73%)
  Pallas kernels  40.3 us (16%)
  between operations  13.4 us (5%)
  starting transfers between devices  9.81 us (4%)
  local copies, waits for them, and re-layouts  4.94 us (2%)
    all_gather x1, waiting for transfers between devices, gather_factors(): over_ctx = lax.all_gather(mine, 'ctx', axis=0)  89.5 us
    all_to_all x1, waiting for transfers between devices, body(): lax.all_to_all(stacked, 'ctx', split_axis=0, concat_axis=0, tiled=True)  71.1 us
    all_to_all x1, waiting for transfers between devices, body(): lax.all_to_all(attended.reshape(heads, tok_rows, HEAD_DIM), 'ctx', split_...  28.7 us
    pallas_call x1, Pallas kernels, attend(): pl.pallas_call(flash_kernel, grid_spec=pltpu.PrefetchScalarGridSpec(num_s...  26.1 us
    pallas_call x1, Pallas kernels, project(): pl.pallas_call(proj_kernel, grid=(PHM_N,), in_specs=[pl.BlockSpec(memory_...  10.9 us
    all_to_all x1, starting transfers between devices, body(): lax.all_to_all(stacked, 'ctx', split_axis=0, concat_axis=0, tiled=True)  5.72 us
  transfers between devices with their start and end apart: 4, of which 3 were waited for; matrix products, arithmetic and copies ran while one was open for 1% of the time, Pallas kernels for 11%

profile of v3, /device:TPU:2, one launch (start us, length us, event | category | flops | bytes accessed | tf_op | source)
XLA Modules:
  0.0 258.6 jit_solution(13010232841604326233)
XLA Ops:
  6.5 0.0 copy-start
  6.5 0.0 all-gather.5.cloned.1.call-start
  6.5 1.0 copy-done
  7.5 0.7 constant_dynamic-slice_fusion
  8.2 0.0 all-gather.5.cloned.1.call-update
  8.2 0.0 all-gather.7.cloned.1.call-start
  8.3 89.5 %all-gather.5.cloned.1.call-done = bf16[2048,1280]{1,0:T(8,128)(2,1)} async-done(((bf16[64,1280]{1,0:T(8,128)(2,1)}), bf16[2048,1280]{1,0:T(8,128)(2,1)}) %all-gather.5.cloned.1.call-update) | async-done | bytes 5242896 | tf_op jit(solution)/shard_map/all_gather | solution.py:176
  97.8 0.0 all-gather.7.cloned.1.call-update
  97.8 3.3 %shard_map.64 = bf16[32,3,128,128]{3,2,1,0:T(8,128)(2,1)} custom-call(bf16[128,4096]{1,0:T(8,128)(2,1)} %q_ref.1, bf16[128,4096]{1,0:T(8,128)(2,1)} %k_ref.1, bf16[128,4096]{1,0:T(8,128)(2,1)} %v_ref.1), custom_call_target="tpu_custom_call" | custom-call | tf_op jit(solution)/shard_map/pallas_call | solution.py:112
  101.1 0.0 copy-start.4
  101.1 5.7 %all-to-all-start = ((bf16[32,3,128,128]{3,2,1,0:T(8,128)(2,1)}), bf16[32,3,128,128]{3,2,1,0:T(8,128)(2,1)S(1)}, u32[]{:S(2)}, u32[]{:S(2)}) async-start(bf16[32,3,128,128]{3,2,1,0:T(8,128)(2,1)} %shard_map.64), calls=%async_computation | async-start | bytes 6291456 | tf_op jit(solution)/shard_map/all_to_all | solution.py:185
  106.9 0.0 copy-done.4
  106.9 0.7 reduce-window.9
  107.6 71.1 %all-to-all-done.q_ref.k_ref.v_ref = bf16[32,3,128,128]{3,2,1,0:T(8,128)(2,1)S(1)} async-done(((bf16[32,3,128,128]{3,2,1,0:T(8,128)(2,1)}), bf16[32,3,128,128]{3,2,1,0:T(8,128)(2,1)S(1)}, u32[]{:S(2)}, u32[]{:S(2)}) %all-to-all-start) | async-done | bytes 3145760 | tf_op jit(solution)/shard_map/all_to_all | solution.py:185
  178.7 0.0 copy-start.1
  178.7 1.6 copy-done.1
  180.4 0.0 copy-start.3
  180.4 26.1 %shard_map.65 = bf16[4096,128]{1,0:T(8,128)(2,1)} custom-call(s32[3]{0:T(128)} %bitcast.9, bf16[32,3,128,128]{3,2,1,0:T(8,128)(2,1)} %copy-done.1, bf16[32,3,128,128]{3,2,1,0:T(8,128)(2,1)} %copy-done.1, bf16[32,3,128,128]{3,2,1,0:T(8,128)(2,1)} %copy-done.1), custom_call_target="tpu_custom_call" | custom-call | tf_op jit(solution)/shard_map/pallas_call | solution.py:84
  206.4 4.0 %all-to-all-start.1 = ((bf16[32,128,128]{2,1,0:T(8,128)(2,1)}), bf16[32,128,128]{2,1,0:T(8,128)(2,1)S(1)}, u32[]{:S(2)}, u32[]{:S(2)}) async-start(bf16[32,128,128]{2,1,0:T(8,128)(2,1)} %bitcast.8), calls=%async_computation.1 | async-start | bytes 2097152 | tf_op jit(solution)/shard_map/all_to_all | solution.py:188
  210.5 0.0 copy-done.3
  210.5 0.7 reshape.32.mix_ref
  211.2 28.7 %all-to-all-done.1.att_ref = bf16[32,128,128]{2,1,0:T(8,128)(2,1)S(1)} async-done(((bf16[32,128,128]{2,1,0:T(8,128)(2,1)}), bf16[32,128,128]{2,1,0:T(8,128)(2,1)S(1)}, u32[]{:S(2)}, u32[]{:S(2)}) %all-to-all-start.1) | async-done | bytes 1048608 | tf_op jit(solution)/shard_map/all_to_all | solution.py:188
  239.8 0.0 copy-start.2
  239.8 0.0 all-gather.7.cloned.1.call-done
  239.8 1.0 copy-done.2
  240.8 10.9 %shard_map.66 = bf16[128,5120]{1,0:T(8,128)(2,1)} custom-call(f32[64]{0:T(128)} %reshape.32.mix_ref, bf16[32,128,128]{2,1,0:T(8,128)(2,1)} %copy-done.2, bf16[2,32,64,1280]{3,2,1,0:T(8,128)(2,1)} %bitcast.6), custom_call_target="tpu_custom_call" | custom-call | tf_op jit(solution)/shard_map/pallas_call | solution.py:154
  (1 shorter events, 0.0 us)
Async XLA Ops:
  6.5 1.0 copy-start
  6.5 91.3 %all-gather.5.cloned.1.call-start = ((), (), s32[]{:S(2)}) async-start(), calls=%async_computation.2 | async-start | bytes 5406720 | tf_op jit(solution)/shard_map/all_gather | solution.py:176
  8.2 231.6 %all-gather.7.cloned.1.call-start = ((), (), s32[]{:S(2)}) async-start(), calls=%async_computation.3 | async-start | bytes 15728640 | tf_op jit(solution)/shard_map/all_gather | solution.py:177
  101.1 5.7 %copy-start.4 = (s32[3]{0:T(128)S(1)}, s32[3]{0:T(128)}, u32[]{:S(2)}) copy-start(s32[3]{0:T(128)} %param.9) | copy-start | bytes 40
  101.1 77.6 %all-to-all-start = ((bf16[32,3,128,128]{3,2,1,0:T(8,128)(2,1)}), bf16[32,3,128,128]{3,2,1,0:T(8,128)(2,1)S(1)}, u32[]{:S(2)}, u32[]{:S(2)}) async-start(bf16[32,3,128,128]{3,2,1,0:T(8,128)(2,1)} %shard_map.64), calls=%async_computation | async-start | bytes 6291456 | tf_op jit(solution)/shard_map/all_to_all | solution.py:185
  178.7 1.6 copy-start.1
  180.4 30.1 %copy-start.3 = (f32[4,4,4]{2,1,0:T(4,128)S(1)}, f32[4,4,4]{2,1,0:T(4,128)}, u32[]{:S(2)}) copy-start(f32[4,4,4]{2,1,0:T(4,128)} %param.10) | copy-start | bytes 772
  206.4 33.4 %all-to-all-start.1 = ((bf16[32,128,128]{2,1,0:T(8,128)(2,1)}), bf16[32,128,128]{2,1,0:T(8,128)(2,1)S(1)}, u32[]{:S(2)}, u32[]{:S(2)}) async-start(bf16[32,128,128]{2,1,0:T(8,128)(2,1)} %bitcast.8), calls=%async_computation.1 | async-start | bytes 2097152 | tf_op jit(solution)/shard_map/all_to_all | solution.py:188
  239.8 1.0 copy-start.2
Sparse Core Ops, SparseCore 0:
  9.9 87.8 all-gather.4
  99.6 25.0 all-gather.6
